TPU v7x, 512 devices: a whole 4x8x8 slice. The times are simulated.
512 devices in a mesh: seq: 64 (over x, z, y_lo), head: 8 (over y_hi, core).
Axes of the slice: x: 4, y: 8 (y_hi: 4, y_lo: 2; y = y_hi * 2 + y_lo), z: 8, core: 2. Of those that a mesh axis runs over, the one named last changes fastest.
Arguments:
- queries: bfloat16 [8192, 8192], P('seq', 'head'), may hold values from -14 to 14, as said below
- key_tokens: bfloat16 [8192, 1024], P(('seq', 'head')), may hold values from -6 to 6, as said below
- value_tokens: bfloat16 [8192, 1024], P(('seq', 'head')), may hold values from -6 to 6
- key_scales: bfloat16 [128, 8], P('seq', 'head'), may hold values from 0.25 to 2.5
- value_scales: bfloat16 [128, 8], P('seq', 'head'), may hold values from 0.25 to 2.5
- value_means: float32 [1024], P('head'), may hold values from -4 to 4
- doc_lengths: int32 [64], replicated, may hold values from 1 to 5120, 8192 in all
Outputs:
- attended: bfloat16 [8192, 8192], P('seq', 'head')
Inputs may be any that keep to these rules, and one draw needn't show every extreme that they name: `doc_lengths`: positive lengths of the documents in order; they sum to 8192, and the longest has exactly 5120 tokens. `queries`: finite values. `key_tokens`: finite values.
All inputs are finite; a program needn't handle non-finite values.
Results may differ from a plain program's by a relative error of at most 0.002.
Values may be sent and summed in bfloat16 or wider, within the bound.
No kernel may reach another device: no remote copies, remote signals or barrier semaphores. Data moves between devices by JAX's collectives and lax.ppermute only.
A program may use at most 64 MiB of HBM per device.

v0:
```python
import math
import jax
import jax.numpy as jnp
from jax import lax
from jax.sharding import PartitionSpec as P

QH = 64
KVH = 8
HD = 128
BLK = 64
NEG = -1e30


def doc_index(positions, starts):
    return jnp.sum((starts[None, :] <= positions[:, None]).astype(jnp.int32), axis=1) - 1


def block_update(
    totals,
    query_tile,
    query_pos,
    query_doc,
    key_tile,
    value_tile,
    key_scale,
    value_scale,
    key_pos,
    starts,
):
    inv_scale = 1.0 / math.sqrt(HD)
    key_doc = doc_index(key_pos, starts)
    allowed = (key_doc[None, :] == query_doc[:, None]) & (key_pos[None, :] <= query_pos[:, None])

    def update(current):
        run_max, run_sum, accumulate = current
        scores = jnp.einsum(
            "kgrd,nkd->kgrn", query_tile, key_tile, preferred_element_type=jnp.float32
        )
        scores = scores * (key_scale.T * inv_scale)[:, None, None, :]
        scores = jnp.where(allowed[None, None], scores, NEG)
        new_max = jnp.maximum(run_max, jnp.max(scores, axis=-1))
        weights = jnp.where(allowed[None, None], jnp.exp(scores - new_max[..., None]), 0.0)
        factor = jnp.exp(run_max - new_max)
        run_sum = run_sum * factor + jnp.sum(weights, axis=-1)
        scaled = (weights * value_scale.T[:, None, None, :]).astype(jnp.bfloat16)
        accumulate = accumulate * factor[..., None] + jnp.einsum(
            "kgrn,nkd->kgrd", scaled, value_tile, preferred_element_type=jnp.float32
        )
        return (new_max, run_sum, accumulate)

    def keep_state(current):
        return current

    return lax.cond(jnp.any(allowed), update, keep_state, totals)


def fold_packet(totals, packet, query_tile, query_pos, query_doc, starts, heads_kv):
    block_count = packet.shape[0]
    sub_blocks = math.gcd(block_count, max(1, 256 // BLK))
    step_count = block_count // sub_blocks
    key_count = sub_blocks * BLK
    key_part = packet[:, 0, :BLK, :].reshape(step_count, key_count, heads_kv, HD)
    value_part = packet[:, 1, :BLK, :].reshape(step_count, key_count, heads_kv, HD)
    key_scale = packet[:, 0, BLK, :].reshape(block_count, heads_kv, HD)[:, :, 0].astype(jnp.float32)
    value_scale = (
        packet[:, 1, BLK, :].reshape(block_count, heads_kv, HD)[:, :, 0].astype(jnp.float32)
    )
    key_scale = jnp.repeat(key_scale, BLK, axis=0).reshape(step_count, key_count, heads_kv)
    value_scale = jnp.repeat(value_scale, BLK, axis=0).reshape(step_count, key_count, heads_kv)
    offsets = jnp.arange(step_count, dtype=jnp.int32) * key_count

    def one_step(current, scan_item):
        key_tile, value_tile, key_sc, value_sc, offset = scan_item
        key_pos = offset + jnp.arange(key_count, dtype=jnp.int32)
        return (
            block_update(
                current,
                query_tile,
                query_pos,
                query_doc,
                key_tile,
                value_tile,
                key_sc,
                value_sc,
                key_pos,
                starts,
            ),
            None,
        )

    totals, _ = lax.scan(one_step, totals, (key_part, value_part, key_scale, value_scale, offsets))
    return totals


def finish(totals, value_means, heads_kv, group_size, row_count):
    run_max, run_sum, accumulate = totals
    result = accumulate / run_sum[..., None] + value_means.reshape(heads_kv, 1, 1, HD)
    return (
        result.transpose(2, 0, 1, 3)
        .reshape(row_count, heads_kv * group_size * HD)
        .astype(jnp.bfloat16)
    )


def shards(queries, key_tokens, value_tokens, key_scales, value_scales, value_means, doc_lengths):
    local_keys, local_values = (
        lax.all_to_all(key_tokens, "head", split_axis=1, concat_axis=0, tiled=True),
        lax.all_to_all(value_tokens, "head", split_axis=1, concat_axis=0, tiled=True),
    )
    row_count = local_keys.shape[0]
    heads_kv = local_keys.shape[1] // HD
    group_size = QH // KVH
    blocks = row_count // BLK
    seq_index = lax.axis_index("seq")
    starts = jnp.cumsum(doc_lengths) - doc_lengths
    key_rows = jnp.concatenate(
        [
            local_keys.reshape(blocks, BLK, heads_kv * HD),
            jnp.repeat(key_scales, HD, axis=1)[:, None, :],
        ],
        axis=1,
    )
    value_rows = jnp.concatenate(
        [
            local_values.reshape(blocks, BLK, heads_kv * HD),
            jnp.repeat(value_scales, HD, axis=1)[:, None, :],
        ],
        axis=1,
    )
    bundle = jnp.stack([key_rows, value_rows], axis=1)

    def prepare(query_rows, query_pos):
        query_tile = query_rows.reshape(query_rows.shape[0], heads_kv, group_size, HD).transpose(
            1, 2, 0, 3
        )
        query_doc = doc_index(query_pos, starts)
        count_rows = query_rows.shape[0]
        initial = (
            jnp.full((heads_kv, group_size, count_rows), NEG, jnp.float32),
            jnp.zeros((heads_kv, group_size, count_rows), jnp.float32),
            jnp.zeros((heads_kv, group_size, count_rows, HD), jnp.float32),
        )

        def folder(totals, packet, first_block):
            return fold_packet(totals, packet, query_tile, query_pos, query_doc, starts, heads_kv)

        return (folder, initial)

    own_pos = seq_index * row_count + jnp.arange(row_count, dtype=jnp.int32)
    folder, initial = prepare(queries, own_pos)
    totals = folder(initial, lax.all_gather(bundle, "seq", axis=0, tiled=True), jnp.int32(0))
    attended = finish(totals, value_means, heads_kv, group_size, row_count)
    return attended


def solution(mesh):
    in_specs = (
        P("seq", "head"),
        P(("seq", "head"), None),
        P(("seq", "head"), None),
        P("seq", "head"),
        P("seq", "head"),
        P("head"),
        P(),
    )
    out_specs = P("seq", "head")
    return jax.shard_map(shards, mesh=mesh, in_specs=in_specs, out_specs=out_specs, check_vma=False)
```

profile of v0, /device:TPU:262, one launch (start us, length us, event | category | flops | bytes accessed | tf_op | source)
XLA Modules:
  0.0 488.3 jit_solution(16897507009504821495)
XLA Ops:
  7.9 7.1 %all-to-all-start = ((bf16[16,8,128]{2,0,1:T(8,128)(2,1)}), bf16[16,8,128]{2,0,1:T(8,128)(2,1)S(1)}, u32[]{:S(2)}, u32[]{:S(2)}) async-start(bf16[16,8,128]{2,0,1:T(8,128)(2,1)} %copy_bitcast_fusion.2), calls=%async_computation | async-start | bytes 65536 | tf_op jit(solution)/shard_map/all_to_all | solution.py:107
  15.0 1.4 copy_bitcast_fusion.1
  17.9 5.0 %all-to-all-done = bf16[16,8,128]{2,0,1:T(8,128)(2,1)S(1)} async-done(((bf16[16,8,128]{2,0,1:T(8,128)(2,1)}), bf16[16,8,128]{2,0,1:T(8,128)(2,1)S(1)}, u32[]{:S(2)}, u32[]{:S(2)}) %all-to-all-start) | async-done | bytes 32800 | tf_op jit(solution)/shard_map/all_to_all | solution.py:107
  22.9 3.3 all-to-all-start.1
  26.4 7.7 %all-to-all-done.1 = bf16[16,8,128]{2,0,1:T(8,128)(2,1)S(1)} async-done(((bf16[16,8,128]{2,0,1:T(8,128)(2,1)}), bf16[16,8,128]{2,0,1:T(8,128)(2,1)S(1)}, u32[]{:S(2)}, u32[]{:S(2)}) %all-to-all-start.1) | async-done | bytes 32800 | tf_op jit(solution)/shard_map/all_to_all | solution.py:108
  38.0 295.4 %all-gather.2.cloned.1.call-done = bf16[128,2,65,128]{3,2,0,1:T(8,128)(2,1)} async-done(((bf16[2,2,65,128]{3,2,0,1:T(8,128)(2,1)}), bf16[128,2,65,128]{3,2,0,1:T(8,128)(2,1)}) %all-gather.2.cloned.1.call-update) | async-done | bytes 4259856 | tf_op jit(solution)/shard_map/all_gather | solution.py:151
  335.0 4.6 fusion.28
  339.6 140.6 %while.17 = (s32[]{:T(128)}, f32[1,8,128]{2,1,0:T(8,128)S(1)}, f32[1,8,128]{2,1,0:T(8,128)S(1)}, f32[1,8,128,128]{3,2,1,0:T(8,128)S(1)}, s32[64]{0:T(128)S(1)}, ...) while((s32[]{:T(128)}, f32[1,8,128]{2,1,0:T(8,128)S(1)}, ...), condition=%wide.region_9.10_spmd.clone, body=%wide.region_2.9_spmd.clone.sunk | while | flops 137285248 | bytes 4997679 | solution.py:91
  364.9 2.4 conditional.3
  365.4 1.2 fusion.26
  370.2 2.4 conditional.3
  370.6 1.1 fusion.26
  375.4 2.4 conditional.3
  375.8 1.1 fusion.26
  380.6 2.4 conditional.3
  385.8 2.4 conditional.3
  391.0 2.4 conditional.3
  396.3 2.4 conditional.3
  401.5 2.4 conditional.3
  406.7 2.4 conditional.3
  411.9 2.4 conditional.3
  417.2 2.4 conditional.3
  422.4 2.4 conditional.3
  427.6 2.4 conditional.3
  432.8 2.4 conditional.3
  438.0 2.4 conditional.3
  443.3 2.4 conditional.3
  448.5 2.4 conditional.3
  453.7 2.4 conditional.3
  458.9 2.4 conditional.3
  464.1 2.4 conditional.3
  469.4 2.4 conditional.3
  (467 shorter events, 122.5 us)
Async XLA Ops:
  6.5 0.8 copy-start
  7.9 15.0 %all-to-all-start = ((bf16[16,8,128]{2,0,1:T(8,128)(2,1)}), bf16[16,8,128]{2,0,1:T(8,128)(2,1)S(1)}, u32[]{:S(2)}, u32[]{:S(2)}) async-start(bf16[16,8,128]{2,0,1:T(8,128)(2,1)} %copy_bitcast_fusion.2), calls=%async_computation | async-start | bytes 65536 | tf_op jit(solution)/shard_map/all_to_all | solution.py:107
  22.9 11.2 %all-to-all-start.1 = ((bf16[16,8,128]{2,0,1:T(8,128)(2,1)}), bf16[16,8,128]{2,0,1:T(8,128)(2,1)S(1)}, u32[]{:S(2)}, u32[]{:S(2)}) async-start(bf16[16,8,128]{2,0,1:T(8,128)(2,1)} %copy_bitcast_fusion.1), calls=%async_computation.1 | async-start | bytes 65536 | tf_op jit(solution)/shard_map/all_to_all | solution.py:108
  26.3 307.1 %all-gather.2.cloned.1.call-start = ((), (), s32[]{:S(2)}) async-start(), calls=%async_computation.2 | async-start | bytes 4792320 | tf_op jit(solution)/shard_map/all_gather | solution.py:151
  339.6 140.6 %copy-start.1 = (f32[128]{0:T(128)S(1)}, f32[128]{0:T(128)}, u32[]{:S(2)}) copy-start(f32[128]{0:T(128)} %param.16) | copy-start | bytes 1540
Sparse Core Ops, SparseCore 0:
  35.0 298.3 all-gather.1
where the time goes:
time: 490 us; the launch traced here: 488 us
  waiting for transfers between devices  308 us (63%)
  other arithmetic  57 us (12%)
  local copies, waits for them, and re-layouts  38.9 us (8%)
  matrix products  35.8 us (7%)
  loops' own time  24.4 us (5%)
  between operations  13.5 us (3%)
  starting transfers between devices  10.5 us (2%)
    all_gather x1, waiting for transfers between devices, shards(): lax.all_gather(bundle, 'seq', axis=0, tiled=True)  295 us
    reduce_or x32, other arithmetic, block_update(): return lax.cond(jnp.any(allowed), update, keep_state, totals)  24.6 us
    dot_general x21, matrix products, update(): jnp.einsum('kgrd,nkd->kgrn', query_tile, key_tile, preferred_element_type...  24.1 us
    another operation x1, loops' own time, fold_packet(): lax.scan(one_step, totals, (key_part, value_part, key_scale, value_scale,...  22.2 us
    add x32, other arithmetic, one_step(): key_pos = offset + jnp.arange(key_count, dtype=jnp.int32)  20.7 us
    dynamic_slice x32, local copies, waits for them, and re-layouts, fold_packet(): lax.scan(one_step, totals, (key_part, value_part, key_scale, value_scale,...  18.8 us
    dot_general x21, matrix products, update(): jnp.einsum('kgrn,nkd->kgrd', scaled, value_tile, preferred_element_type=j...  11.6 us
  transfers between devices with their start and end apart: 3, of which 3 were waited for; matrix products, arithmetic and copies ran while one was open for 1% of the time, Pallas kernels for 0%

commit v1 on v0

--- a/solution.py
+++ b/solution.py
@@ -148,7 +148,13 @@
 
     own_pos = seq_index * row_count + jnp.arange(row_count, dtype=jnp.int32)
     folder, initial = prepare(queries, own_pos)
-    totals = folder(initial, lax.all_gather(bundle, "seq", axis=0, tiled=True), jnp.int32(0))
+    totals = folder(
+        initial,
+        jnp.concatenate(
+            lax.all_to_all(jnp.stack([bundle] * lax.axis_size("seq")), "seq", 0, 0), axis=0
+        ),
+        jnp.int32(0),
+    )
     attended = finish(totals, value_means, heads_kv, group_size, row_count)
     return attended
 

time: 490 us -> 316 us (0.64)
  the two profiles are of different devices: /device:TPU:262 before, /device:TPU:206 now
where the time goes in v1:
time: 316 us; the launch traced here: 313 us
  waiting for transfers between devices  108 us (34%)
  other arithmetic  54.7 us (17%)
  local copies, waits for them, and re-layouts  52.4 us (17%)
  matrix products  51.8 us (16%)
  loops' own time  23.3 us (7%)
  starting transfers between devices  22.1 us (7%)
    all_to_all x1, waiting for transfers between devices, shards(): lax.all_to_all(jnp.stack([bundle] * lax.axis_size('seq')), 'seq', 0, 0)  95.3 us
    dot_general x20, matrix products, update(): jnp.einsum('kgrn,nkd->kgrd', scaled, value_tile, preferred_element_type=j...  28.6 us
    reduce_or x32, other arithmetic, block_update(): return lax.cond(jnp.any(allowed), update, keep_state, totals)  24.8 us
    dot_general x20, matrix products, update(): jnp.einsum('kgrd,nkd->kgrn', query_tile, key_tile, preferred_element_type...  23.2 us
    another operation x1, loops' own time, fold_packet(): lax.scan(one_step, totals, (key_part, value_part, key_scale, value_scale,...  21.2 us
    add x32, other arithmetic, one_step(): key_pos = offset + jnp.arange(key_count, dtype=jnp.int32)  19.8 us
    dynamic_slice x32, local copies, waits for them, and re-layouts, fold_packet(): lax.scan(one_step, totals, (key_part, value_part, key_scale, value_scale,...  19 us
    all_to_all x1, starting transfers between devices, shards(): lax.all_to_all(jnp.stack([bundle] * lax.axis_size('seq')), 'seq', 0, 0)  12.5 us
  transfers between devices with their start and end apart: 3, of which 3 were waited for; matrix products, arithmetic and copies ran while one was open for 1% of the time, Pallas kernels for 0%

profile of v1, /device:TPU:206, one launch (start us, length us, event | category | flops | bytes accessed | tf_op | source)
XLA Modules:
  0.0 312.6 jit_solution(17232475648404223032)
XLA Ops:
  1.4 6.2 %all-to-all-start = ((bf16[16,8,128]{2,0,1:T(8,128)(2,1)}), bf16[16,8,128]{2,0,1:T(8,128)(2,1)S(1)}, u32[]{:S(2)}, u32[]{:S(2)}) async-start(bf16[16,8,128]{2,0,1:T(8,128)(2,1)} %copy_bitcast_fusion.2), calls=%async_computation | async-start | bytes 65536 | tf_op jit(solution)/shard_map/all_to_all | solution.py:107
  10.5 5.0 %all-to-all-done = bf16[16,8,128]{2,0,1:T(8,128)(2,1)S(1)} async-done(((bf16[16,8,128]{2,0,1:T(8,128)(2,1)}), bf16[16,8,128]{2,0,1:T(8,128)(2,1)S(1)}, u32[]{:S(2)}, u32[]{:S(2)}) %all-to-all-start) | async-done | bytes 32800 | tf_op jit(solution)/shard_map/all_to_all | solution.py:107
  15.5 3.3 %all-to-all-start.1 = ((bf16[16,8,128]{2,0,1:T(8,128)(2,1)}), bf16[16,8,128]{2,0,1:T(8,128)(2,1)S(1)}, u32[]{:S(2)}, u32[]{:S(2)}) async-start(bf16[16,8,128]{2,0,1:T(8,128)(2,1)} %copy_bitcast_fusion.1), calls=%async_computation.1 | async-start | bytes 65536 | tf_op jit(solution)/shard_map/all_to_all | solution.py:108
  18.9 7.8 %all-to-all-done.1 = bf16[16,8,128]{2,0,1:T(8,128)(2,1)S(1)} async-done(((bf16[16,8,128]{2,0,1:T(8,128)(2,1)}), bf16[16,8,128]{2,0,1:T(8,128)(2,1)S(1)}, u32[]{:S(2)}, u32[]{:S(2)}) %all-to-all-start.1) | async-done | bytes 32800 | tf_op jit(solution)/shard_map/all_to_all | solution.py:108
  26.9 4.2 %stack.11 = bf16[64,2,2,65,128]{4,1,3,2,0:T(2,128)(2,1)} broadcast(bf16[2,2,65,128]{3,0,2,1:T(2,128)(2,1)S(1)} %copy.48), dimensions={1,2,3,4} | broadcast | bytes 4326400 | tf_op jit(solution)/shard_map/stack | solution.py:154
  31.1 12.5 %all-to-all-start.2 = ((bf16[64,2,2,65,128]{4,1,3,2,0:T(2,128)(2,1)}), bf16[64,2,2,65,128]{4,1,3,2,0:T(2,128)(2,1)}, u32[]{:S(2)}, u32[]{:S(2)}) async-start(bf16[64,2,2,65,128]{4,1,3,2,0:T(2,128)(2,1)} %stack.11), calls=%async_computation.2 | async-start | bytes 8519680 | tf_op jit(solution)/shard_map/all_to_all | solution.py:154
  44.5 95.3 %all-to-all-done.2 = bf16[64,2,2,65,128]{4,1,3,2,0:T(2,128)(2,1)} async-done(((bf16[64,2,2,65,128]{4,1,3,2,0:T(2,128)(2,1)}), bf16[64,2,2,65,128]{4,1,3,2,0:T(2,128)(2,1)}, u32[]{:S(2)}, u32[]{:S(2)}) %all-to-all-start.2) | async-done | bytes 4259872 | tf_op jit(solution)/shard_map/all_to_all | solution.py:154
  139.8 7.0 %copy.49 = bf16[64,2,2,65,128]{4,1,0,3,2:T(2,128)(2,1)S(1)} copy(bf16[64,2,2,65,128]{4,1,3,2,0:T(2,128)(2,1)} %all-to-all-done.2) | data formatting | bytes 8519680 | tf_op jit(solution)/shard_map/all_to_all | solution.py:154
  146.8 2.5 fusion.27
  149.7 4.4 %copy.50 = bf16[128,1,64,128]{3,2,0,1:T(8,128)(2,1)} copy(bf16[128,1,64,128]{3,0,2,1:T(8,128)(2,1)} %get-tuple-element.406) | data formatting | bytes 4194304 | tf_op jit(solution)/shard_map/slice | solution.py:62
  154.1 2.6 copy.52
  156.9 154.5 %while.17 = (s32[]{:T(128)}, f32[1,8,128]{2,1,0:T(8,128)S(1)}, f32[1,8,128]{2,1,0:T(8,128)S(1)}, f32[1,8,128,128]{3,2,1,0:T(8,128)S(1)}, s32[64]{0:T(128)S(1)}, ...) while((s32[]{:T(128)}, f32[1,8,128]{2,1,0:T(8,128)S(1)}, ...), condition=%wide.region_9.10_spmd.clone, body=%wide.region_2.9_spmd.clone.sunk | while | flops 137285248 | bytes 4998187 | solution.py:91
  181.8 3.3 %conditional.3 = ((f32[1,8,128]{2,1,0:T(8,128)S(1)}, f32[1,8,128]{2,1,0:T(8,128)S(1)}, f32[1,8,128,128]{3,2,1,0:T(8,128)S(1)})) conditional(s32[]{:T(128)} %convert_element_type.74, (f32[1,8,128]{2,1,0:T(8,128)S(1)}, f32[1,8,128]{2,1,0:T(8,128)S(1)}, f32[1,8,128,128]{3,2,1,0:T(8,128)S(1)}) %tuple.59, (pred[128,256]{0,1:T(8,128)(4,1)S(1)}, ...), branch_computations={%region_5.5_spmd, %region_6.8_spmd} | conditional | flops 137104640 | bytes 4956196 | solution.py:54
  187.9 3.3 %conditional.3 = ((f32[1,8,128]{2,1,0:T(8,128)S(1)}, f32[1,8,128]{2,1,0:T(8,128)S(1)}, f32[1,8,128,128]{3,2,1,0:T(8,128)S(1)})) conditional(s32[]{:T(128)} %convert_element_type.74, (f32[1,8,128]{2,1,0:T(8,128)S(1)}, f32[1,8,128]{2,1,0:T(8,128)S(1)}, f32[1,8,128,128]{3,2,1,0:T(8,128)S(1)}) %tuple.59, (pred[128,256]{0,1:T(8,128)(4,1)S(1)}, ...), branch_computations={%region_5.5_spmd, %region_6.8_spmd} | conditional | flops 137104640 | bytes 4956196 | solution.py:54
  193.9 3.3 %conditional.3 = ((f32[1,8,128]{2,1,0:T(8,128)S(1)}, f32[1,8,128]{2,1,0:T(8,128)S(1)}, f32[1,8,128,128]{3,2,1,0:T(8,128)S(1)})) conditional(s32[]{:T(128)} %convert_element_type.74, (f32[1,8,128]{2,1,0:T(8,128)S(1)}, f32[1,8,128]{2,1,0:T(8,128)S(1)}, f32[1,8,128,128]{3,2,1,0:T(8,128)S(1)}) %tuple.59, (pred[128,256]{0,1:T(8,128)(4,1)S(1)}, ...), branch_computations={%region_5.5_spmd, %region_6.8_spmd} | conditional | flops 137104640 | bytes 4956196 | solution.py:54
  200.0 3.3 %conditional.3 = ((f32[1,8,128]{2,1,0:T(8,128)S(1)}, f32[1,8,128]{2,1,0:T(8,128)S(1)}, f32[1,8,128,128]{3,2,1,0:T(8,128)S(1)})) conditional(s32[]{:T(128)} %convert_element_type.74, (f32[1,8,128]{2,1,0:T(8,128)S(1)}, f32[1,8,128]{2,1,0:T(8,128)S(1)}, f32[1,8,128,128]{3,2,1,0:T(8,128)S(1)}) %tuple.59, (pred[128,256]{0,1:T(8,128)(4,1)S(1)}, ...), branch_computations={%region_5.5_spmd, %region_6.8_spmd} | conditional | flops 137104640 | bytes 4956196 | solution.py:54
  206.0 3.3 %conditional.3 = ((f32[1,8,128]{2,1,0:T(8,128)S(1)}, f32[1,8,128]{2,1,0:T(8,128)S(1)}, f32[1,8,128,128]{3,2,1,0:T(8,128)S(1)})) conditional(s32[]{:T(128)} %convert_element_type.74, (f32[1,8,128]{2,1,0:T(8,128)S(1)}, f32[1,8,128]{2,1,0:T(8,128)S(1)}, f32[1,8,128,128]{3,2,1,0:T(8,128)S(1)}) %tuple.59, (pred[128,256]{0,1:T(8,128)(4,1)S(1)}, ...), branch_computations={%region_5.5_spmd, %region_6.8_spmd} | conditional | flops 137104640 | bytes 4956196 | solution.py:54
  212.1 3.3 %conditional.3 = ((f32[1,8,128]{2,1,0:T(8,128)S(1)}, f32[1,8,128]{2,1,0:T(8,128)S(1)}, f32[1,8,128,128]{3,2,1,0:T(8,128)S(1)})) conditional(s32[]{:T(128)} %convert_element_type.74, (f32[1,8,128]{2,1,0:T(8,128)S(1)}, f32[1,8,128]{2,1,0:T(8,128)S(1)}, f32[1,8,128,128]{3,2,1,0:T(8,128)S(1)}) %tuple.59, (pred[128,256]{0,1:T(8,128)(4,1)S(1)}, ...), branch_computations={%region_5.5_spmd, %region_6.8_spmd} | conditional | flops 137104640 | bytes 4956196 | solution.py:54
  218.2 3.3 %conditional.3 = ((f32[1,8,128]{2,1,0:T(8,128)S(1)}, f32[1,8,128]{2,1,0:T(8,128)S(1)}, f32[1,8,128,128]{3,2,1,0:T(8,128)S(1)})) conditional(s32[]{:T(128)} %convert_element_type.74, (f32[1,8,128]{2,1,0:T(8,128)S(1)}, f32[1,8,128]{2,1,0:T(8,128)S(1)}, f32[1,8,128,128]{3,2,1,0:T(8,128)S(1)}) %tuple.59, (pred[128,256]{0,1:T(8,128)(4,1)S(1)}, ...), branch_computations={%region_5.5_spmd, %region_6.8_spmd} | conditional | flops 137104640 | bytes 4956196 | solution.py:54
  224.2 3.3 %conditional.3 = ((f32[1,8,128]{2,1,0:T(8,128)S(1)}, f32[1,8,128]{2,1,0:T(8,128)S(1)}, f32[1,8,128,128]{3,2,1,0:T(8,128)S(1)})) conditional(s32[]{:T(128)} %convert_element_type.74, (f32[1,8,128]{2,1,0:T(8,128)S(1)}, f32[1,8,128]{2,1,0:T(8,128)S(1)}, f32[1,8,128,128]{3,2,1,0:T(8,128)S(1)}) %tuple.59, (pred[128,256]{0,1:T(8,128)(4,1)S(1)}, ...), branch_computations={%region_5.5_spmd, %region_6.8_spmd} | conditional | flops 137104640 | bytes 4956196 | solution.py:54
  230.3 3.3 %conditional.3 = ((f32[1,8,128]{2,1,0:T(8,128)S(1)}, f32[1,8,128]{2,1,0:T(8,128)S(1)}, f32[1,8,128,128]{3,2,1,0:T(8,128)S(1)})) conditional(s32[]{:T(128)} %convert_element_type.74, (f32[1,8,128]{2,1,0:T(8,128)S(1)}, f32[1,8,128]{2,1,0:T(8,128)S(1)}, f32[1,8,128,128]{3,2,1,0:T(8,128)S(1)}) %tuple.59, (pred[128,256]{0,1:T(8,128)(4,1)S(1)}, ...), branch_computations={%region_5.5_spmd, %region_6.8_spmd} | conditional | flops 137104640 | bytes 4956196 | solution.py:54
  236.4 3.3 %conditional.3 = ((f32[1,8,128]{2,1,0:T(8,128)S(1)}, f32[1,8,128]{2,1,0:T(8,128)S(1)}, f32[1,8,128,128]{3,2,1,0:T(8,128)S(1)})) conditional(s32[]{:T(128)} %convert_element_type.74, (f32[1,8,128]{2,1,0:T(8,128)S(1)}, f32[1,8,128]{2,1,0:T(8,128)S(1)}, f32[1,8,128,128]{3,2,1,0:T(8,128)S(1)}) %tuple.59, (pred[128,256]{0,1:T(8,128)(4,1)S(1)}, ...), branch_computations={%region_5.5_spmd, %region_6.8_spmd} | conditional | flops 137104640 | bytes 4956196 | solution.py:54
  242.4 3.3 %conditional.3 = ((f32[1,8,128]{2,1,0:T(8,128)S(1)}, f32[1,8,128]{2,1,0:T(8,128)S(1)}, f32[1,8,128,128]{3,2,1,0:T(8,128)S(1)})) conditional(s32[]{:T(128)} %convert_element_type.74, (f32[1,8,128]{2,1,0:T(8,128)S(1)}, f32[1,8,128]{2,1,0:T(8,128)S(1)}, f32[1,8,128,128]{3,2,1,0:T(8,128)S(1)}) %tuple.59, (pred[128,256]{0,1:T(8,128)(4,1)S(1)}, ...), branch_computations={%region_5.5_spmd, %region_6.8_spmd} | conditional | flops 137104640 | bytes 4956196 | solution.py:54
  248.5 3.3 %conditional.3 = ((f32[1,8,128]{2,1,0:T(8,128)S(1)}, f32[1,8,128]{2,1,0:T(8,128)S(1)}, f32[1,8,128,128]{3,2,1,0:T(8,128)S(1)})) conditional(s32[]{:T(128)} %convert_element_type.74, (f32[1,8,128]{2,1,0:T(8,128)S(1)}, f32[1,8,128]{2,1,0:T(8,128)S(1)}, f32[1,8,128,128]{3,2,1,0:T(8,128)S(1)}) %tuple.59, (pred[128,256]{0,1:T(8,128)(4,1)S(1)}, ...), branch_computations={%region_5.5_spmd, %region_6.8_spmd} | conditional | flops 137104640 | bytes 4956196 | solution.py:54
  254.5 3.3 %conditional.3 = ((f32[1,8,128]{2,1,0:T(8,128)S(1)}, f32[1,8,128]{2,1,0:T(8,128)S(1)}, f32[1,8,128,128]{3,2,1,0:T(8,128)S(1)})) conditional(s32[]{:T(128)} %convert_element_type.74, (f32[1,8,128]{2,1,0:T(8,128)S(1)}, f32[1,8,128]{2,1,0:T(8,128)S(1)}, f32[1,8,128,128]{3,2,1,0:T(8,128)S(1)}) %tuple.59, (pred[128,256]{0,1:T(8,128)(4,1)S(1)}, ...), branch_computations={%region_5.5_spmd, %region_6.8_spmd} | conditional | flops 137104640 | bytes 4956196 | solution.py:54
  260.6 3.3 %conditional.3 = ((f32[1,8,128]{2,1,0:T(8,128)S(1)}, f32[1,8,128]{2,1,0:T(8,128)S(1)}, f32[1,8,128,128]{3,2,1,0:T(8,128)S(1)})) conditional(s32[]{:T(128)} %convert_element_type.74, (f32[1,8,128]{2,1,0:T(8,128)S(1)}, f32[1,8,128]{2,1,0:T(8,128)S(1)}, f32[1,8,128,128]{3,2,1,0:T(8,128)S(1)}) %tuple.59, (pred[128,256]{0,1:T(8,128)(4,1)S(1)}, ...), branch_computations={%region_5.5_spmd, %region_6.8_spmd} | conditional | flops 137104640 | bytes 4956196 | solution.py:54
  266.7 3.3 %conditional.3 = ((f32[1,8,128]{2,1,0:T(8,128)S(1)}, f32[1,8,128]{2,1,0:T(8,128)S(1)}, f32[1,8,128,128]{3,2,1,0:T(8,128)S(1)})) conditional(s32[]{:T(128)} %convert_element_type.74, (f32[1,8,128]{2,1,0:T(8,128)S(1)}, f32[1,8,128]{2,1,0:T(8,128)S(1)}, f32[1,8,128,128]{3,2,1,0:T(8,128)S(1)}) %tuple.59, (pred[128,256]{0,1:T(8,128)(4,1)S(1)}, ...), branch_computations={%region_5.5_spmd, %region_6.8_spmd} | conditional | flops 137104640 | bytes 4956196 | solution.py:54
  272.7 3.3 %conditional.3 = ((f32[1,8,128]{2,1,0:T(8,128)S(1)}, f32[1,8,128]{2,1,0:T(8,128)S(1)}, f32[1,8,128,128]{3,2,1,0:T(8,128)S(1)})) conditional(s32[]{:T(128)} %convert_element_type.74, (f32[1,8,128]{2,1,0:T(8,128)S(1)}, f32[1,8,128]{2,1,0:T(8,128)S(1)}, f32[1,8,128,128]{3,2,1,0:T(8,128)S(1)}) %tuple.59, (pred[128,256]{0,1:T(8,128)(4,1)S(1)}, ...), branch_computations={%region_5.5_spmd, %region_6.8_spmd} | conditional | flops 137104640 | bytes 4956196 | solution.py:54
  278.8 3.3 %conditional.3 = ((f32[1,8,128]{2,1,0:T(8,128)S(1)}, f32[1,8,128]{2,1,0:T(8,128)S(1)}, f32[1,8,128,128]{3,2,1,0:T(8,128)S(1)})) conditional(s32[]{:T(128)} %convert_element_type.74, (f32[1,8,128]{2,1,0:T(8,128)S(1)}, f32[1,8,128]{2,1,0:T(8,128)S(1)}, f32[1,8,128,128]{3,2,1,0:T(8,128)S(1)}) %tuple.59, (pred[128,256]{0,1:T(8,128)(4,1)S(1)}, ...), branch_computations={%region_5.5_spmd, %region_6.8_spmd} | conditional | flops 137104640 | bytes 4956196 | solution.py:54
  284.9 3.3 %conditional.3 = ((f32[1,8,128]{2,1,0:T(8,128)S(1)}, f32[1,8,128]{2,1,0:T(8,128)S(1)}, f32[1,8,128,128]{3,2,1,0:T(8,128)S(1)})) conditional(s32[]{:T(128)} %convert_element_type.74, (f32[1,8,128]{2,1,0:T(8,128)S(1)}, f32[1,8,128]{2,1,0:T(8,128)S(1)}, f32[1,8,128,128]{3,2,1,0:T(8,128)S(1)}) %tuple.59, (pred[128,256]{0,1:T(8,128)(4,1)S(1)}, ...), branch_computations={%region_5.5_spmd, %region_6.8_spmd} | conditional | flops 137104640 | bytes 4956196 | solution.py:54
  290.9 3.3 %conditional.3 = ((f32[1,8,128]{2,1,0:T(8,128)S(1)}, f32[1,8,128]{2,1,0:T(8,128)S(1)}, f32[1,8,128,128]{3,2,1,0:T(8,128)S(1)})) conditional(s32[]{:T(128)} %convert_element_type.74, (f32[1,8,128]{2,1,0:T(8,128)S(1)}, f32[1,8,128]{2,1,0:T(8,128)S(1)}, f32[1,8,128,128]{3,2,1,0:T(8,128)S(1)}) %tuple.59, (pred[128,256]{0,1:T(8,128)(4,1)S(1)}, ...), branch_computations={%region_5.5_spmd, %region_6.8_spmd} | conditional | flops 137104640 | bytes 4956196 | solution.py:54
  297.0 3.3 %conditional.3 = ((f32[1,8,128]{2,1,0:T(8,128)S(1)}, f32[1,8,128]{2,1,0:T(8,128)S(1)}, f32[1,8,128,128]{3,2,1,0:T(8,128)S(1)})) conditional(s32[]{:T(128)} %convert_element_type.74, (f32[1,8,128]{2,1,0:T(8,128)S(1)}, f32[1,8,128]{2,1,0:T(8,128)S(1)}, f32[1,8,128,128]{3,2,1,0:T(8,128)S(1)}) %tuple.59, (pred[128,256]{0,1:T(8,128)(4,1)S(1)}, ...), branch_computations={%region_5.5_spmd, %region_6.8_spmd} | conditional | flops 137104640 | bytes 4956196 | solution.py:54
  (464 shorter events, 138.2 us)
Async XLA Ops:
  0.0 0.8 copy-start
  1.4 14.1 %all-to-all-start = ((bf16[16,8,128]{2,0,1:T(8,128)(2,1)}), bf16[16,8,128]{2,0,1:T(8,128)(2,1)S(1)}, u32[]{:S(2)}, u32[]{:S(2)}) async-start(bf16[16,8,128]{2,0,1:T(8,128)(2,1)} %copy_bitcast_fusion.2), calls=%async_computation | async-start | bytes 65536 | tf_op jit(solution)/shard_map/all_to_all | solution.py:107
  15.5 11.2 %all-to-all-start.1 = ((bf16[16,8,128]{2,0,1:T(8,128)(2,1)}), bf16[16,8,128]{2,0,1:T(8,128)(2,1)S(1)}, u32[]{:S(2)}, u32[]{:S(2)}) async-start(bf16[16,8,128]{2,0,1:T(8,128)(2,1)} %copy_bitcast_fusion.1), calls=%async_computation.1 | async-start | bytes 65536 | tf_op jit(solution)/shard_map/all_to_all | solution.py:108
  31.1 12.6 %copy-start.3 = (s32[64]{0:T(128)S(1)}, s32[64]{0:T(128)}, u32[]{:S(2)}) copy-start(s32[64]{0:T(128)} %param.17) | copy-start | bytes 772
  31.1 12.9 %copy-start.2 = (bf16[128,1024]{1,0:T(8,128)(2,1)S(1)}, bf16[128,1024]{1,0:T(8,128)(2,1)}, u32[]{:S(2)}) copy-start(bf16[128,1024]{1,0:T(8,128)(2,1)} %param.11) | copy-start | bytes 786436
  31.1 108.7 %all-to-all-start.2 = ((bf16[64,2,2,65,128]{4,1,3,2,0:T(2,128)(2,1)}), bf16[64,2,2,65,128]{4,1,3,2,0:T(2,128)(2,1)}, u32[]{:S(2)}, u32[]{:S(2)}) async-start(bf16[64,2,2,65,128]{4,1,3,2,0:T(2,128)(2,1)} %stack.11), calls=%async_computation.2 | async-start | bytes 8519680 | tf_op jit(solution)/shard_map/all_to_all | solution.py:154
  149.7 4.5 %copy-start.1 = (bf16[128,1,64,128]{3,0,2,1:T(8,128)(2,1)S(1)}, bf16[128,1,64,128]{3,0,2,1:T(8,128)(2,1)}, u32[]{:S(2)}) copy-start(bf16[128,1,64,128]{3,0,2,1:T(8,128)(2,1)} %get-tuple-element.405) | copy-start | bytes 6291460
  156.9 154.6 %copy-start.4 = (f32[128]{0:T(128)S(1)}, f32[128]{0:T(128)}, u32[]{:S(2)}) copy-start(f32[128]{0:T(128)} %param.16) | copy-start | bytes 1540
